TPU v7x, 512 devices: a whole 4x4x16 slice. The times are simulated.
512 devices in a mesh: tm: 64 (over z, y), area: 8 (over x, core).
Axes of the slice: x: 4, y: 4, z: 16, core: 2. Of those that a mesh axis runs over, the one named last changes fastest.
Arguments:
- demand: float32 [256, 71680], P('tm', 'area'), may hold values from -6 to 6
- unit_cost: float32 [256, 65536], P('tm', 'area'), may hold values from -18 to 18
- ptdf_tiles: bfloat16 [192, 128, 256], P('area'), may hold values from -0.25 to 0.25
- tile_area: int32 [192, 1], replicated, may hold values from 0 to 7; in each aligned block of 24 rows (0 to 23, 24 to 47, ...) at most 6 rows name the same one
- tile_block: int32 [192], replicated, may hold values from 0 to 34
- tile_row: int32 [192], replicated, may hold values from 0 to 11
- unit_bus: int32 [65536], P('area'), may hold values from 0 to 8959
- unit_class: int32 [65536], P('area'), may hold values from 0 to 2
- power_cap: float32 [65536], P('area'), may hold values from 0.1 to 2
- line_limit: float32 [12288], P('area'), may hold values from 0.2 to 2
- smoother: float32 [3, 256], replicated, as said below
Outputs:
- power: float32 [256, 65536], P('tm', 'area')
- line_duals: float32 [256, 12288], P('tm', 'area')
- primal_rms: float32 [2], replicated
Inputs may be any that keep to these rules, and one draw needn't show every extreme that they name: `tile_area`: among the 24 tiles of one holder, at most 6 have their column block in one area, and some holder reaches 6. `smoother`: row k is the first column of the inverse of (c1 I + L)(c2 I + L) / (c1 c2) of order 256, with L = 2 I - S - S^T the cyclic second difference and class constants 1e-5 <= c1 < c2 <= 1.
All inputs are finite; a program needn't handle non-finite values.
Results may differ from a plain program's by a relative error of at most 0.0028.
Values may be sent and summed in bfloat16 or wider, within the bound.
No kernel may reach another device: no remote copies, remote signals or barrier semaphores. Data moves between devices by JAX's collectives and lax.ppermute only.
A program may use at most 64 MiB of HBM per device.

v0:
```python
import functools
import math
import jax
import jax.numpy as jnp
from jax import lax
from jax.sharding import Mesh
from jax.sharding import PartitionSpec as P

ITERATIONS = 2
TM = ("tm_0", "tm_1")
AREA = ("area_0", "area_1")
TM_AREA = ("tm_0", "tm_1", "area_0", "area_1")
step_size = 0.5
rho_weight = 1.0


def laid_out(tiles, dim):
    dims = list(tiles.shape[1:])
    dims[dim] *= tiles.shape[0]
    return jnp.moveaxis(tiles, 0, dim).reshape(dims)


def copy_for_each(array, axis):
    count = lax.axis_size(axis)
    return lax.all_to_all(
        jnp.broadcast_to(array[None], (count, *array.shape)), axis, 0, 0, tiled=True
    )


def collect(array, axis, dim):
    return laid_out(copy_for_each(array, axis), dim)


def one_axis_at_a_time(array, axes):
    return functools.reduce(lax.psum, axes, array)


def per_device(
    demand,
    unit_cost,
    ptdf_tiles,
    tile_area,
    tile_block,
    tile_row,
    unit_bus,
    unit_class,
    power_cap,
    line_limit,
    smoother,
):
    time_devices = lax.axis_size(TM)
    area_devices = lax.axis_size(AREA)
    block_steps, bus_area = demand.shape
    unit_area = unit_cost.shape[1]
    tile_count, line_block, panel_width = ptdf_tiles.shape
    col_blocks = bus_area // panel_width
    row_blocks = line_limit.shape[0] // line_block
    capacity = 2 * tile_count // area_devices
    horizon = block_steps * time_devices
    unit_width = unit_area // time_devices
    area_index = lax.axis_index(AREA)
    time_index = lax.axis_index(TM)
    tile_areas = tile_area.reshape(area_devices, tile_count)
    block_grid = tile_block.reshape(area_devices, tile_count)
    row_grid = tile_row.reshape(area_devices, tile_count)
    is_source = (tile_areas == area_index).astype(jnp.int32)
    rank_source = jnp.cumsum(is_source, axis=1) - 1
    slot_ids = jnp.arange(capacity, dtype=jnp.int32)
    chosen = is_source[:, None, :] * (rank_source[:, None, :] == slot_ids[None, :, None]).astype(
        jnp.int32
    )
    send_block = jnp.sum(chosen * block_grid[:, None, :], axis=2).reshape(-1)
    my_areas = lax.dynamic_index_in_dim(tile_areas, area_index, 0, keepdims=False)
    my_blocks = lax.dynamic_index_in_dim(block_grid, area_index, 0, keepdims=False)
    my_rows = lax.dynamic_index_in_dim(row_grid, area_index, 0, keepdims=False)
    positions = jnp.arange(tile_count, dtype=jnp.int32)
    earlier = positions[None, :] <= positions[:, None]
    same_area = my_areas[None, :] == my_areas[:, None]
    rank_mine = jnp.sum((same_area & earlier).astype(jnp.int32), axis=1) - 1
    slot_of_tile = my_areas * capacity + rank_mine
    my_columns = my_areas * col_blocks + my_blocks
    my_class = lax.dynamic_slice_in_dim(unit_class, time_index * unit_width, unit_width)
    my_cap = lax.dynamic_slice_in_dim(power_cap, time_index * unit_width, unit_width)
    half_steps = horizon // 2
    steps_line = jnp.arange(horizon, dtype=jnp.int32)
    frequency = jnp.concatenate(
        [jnp.arange(half_steps + 1, dtype=jnp.int32), jnp.arange(1, half_steps, dtype=jnp.int32)]
    )
    angle = (frequency[:, None] * steps_line[None, :] % horizon).astype(jnp.float32) * (
        2.0 * math.pi / horizon
    )
    cosine_rows = (steps_line <= half_steps)[:, None]
    forward = jnp.where(cosine_rows, jnp.cos(angle), -jnp.sin(angle))
    edge_rows = (frequency == 0) | (frequency == half_steps)
    row_weight = (jnp.where(edge_rows, 1.0, 2.0).astype(jnp.float32) / horizon)[:, None]
    kernel_spectrum = jnp.dot(
        forward, smoother.T, precision=lax.Precision.HIGHEST, preferred_element_type=jnp.float32
    )
    class_table = (
        my_class[None, :] == jnp.arange(smoother.shape[0], dtype=jnp.int32)[:, None]
    ).astype(jnp.float32)
    unit_spectrum = jnp.dot(
        kernel_spectrum,
        class_table,
        precision=lax.Precision.HIGHEST,
        preferred_element_type=jnp.float32,
    )
    empty_row = jnp.zeros((1, unit_width), jnp.float32)
    kernel_real = unit_spectrum[: half_steps + 1]
    kernel_imag = jnp.concatenate([empty_row, unit_spectrum[half_steps + 1 :], empty_row], axis=0)
    power_time = jnp.zeros((block_steps, unit_area), jnp.float32)
    line_duals = jnp.zeros((block_steps, line_limit.shape[0]), jnp.float32)
    totals = []
    for repeat in range(ITERATIONS):
        if repeat == 0:
            injection = demand.astype(jnp.bfloat16)
        else:
            injection = demand.at[:, unit_bus].add(power_time).astype(jnp.bfloat16)
        gathered = collect(injection, AREA, 1)
        panels = jnp.take(
            gathered.reshape(block_steps, area_devices * col_blocks, panel_width),
            my_columns,
            axis=1,
        )
        partial_value = jnp.einsum(
            "tjb,jlb->tjl", panels, ptdf_tiles, preferred_element_type=jnp.float32
        )
        line_flows = (
            jnp.zeros((block_steps, row_blocks, line_block), jnp.float32)
            .at[:, my_rows]
            .add(partial_value)
        )
        line_flows = line_flows.reshape(block_steps, row_blocks * line_block)
        limits = line_limit[None, :]
        clipped = jnp.clip(line_flows + line_duals, -limits, limits)
        line_duals = line_duals + line_flows - clipped
        excess = line_flows - clipped
        local_total = jnp.sum(excess * excess)
        totals.append(local_total)
        weights = (line_duals + line_flows - clipped).astype(jnp.bfloat16)
        picked = jnp.take(weights.reshape(block_steps, row_blocks, line_block), my_rows, axis=1)
        contrib = jnp.einsum("tjl,jlb->tjb", picked, ptdf_tiles, preferred_element_type=jnp.float32)
        outbound = (
            jnp.zeros((block_steps, area_devices * capacity, panel_width), jnp.float32)
            .at[:, slot_of_tile]
            .set(contrib)
        )
        outbound = outbound.reshape(block_steps, area_devices, capacity, panel_width)
        returned = lax.all_to_all(outbound, AREA, split_axis=1, concat_axis=1, tiled=True)
        prices = (
            jnp.zeros((block_steps, col_blocks, panel_width), jnp.float32)
            .at[:, send_block]
            .add(returned.reshape(block_steps, area_devices * capacity, panel_width))
        )
        prices = prices.reshape(block_steps, bus_area)
        gradient = unit_cost + rho_weight * jnp.take(prices, unit_bus, axis=1)
        target = power_time - step_size * gradient
        columns = lax.all_to_all(target, TM, split_axis=1, concat_axis=0, tiled=True)
        spectrum = jnp.dot(
            forward, columns, precision=lax.Precision.HIGHEST, preferred_element_type=jnp.float32
        )
        spectrum_real = spectrum[: half_steps + 1]
        spectrum_imag = jnp.concatenate([empty_row, spectrum[half_steps + 1 :], empty_row], axis=0)
        product_real = spectrum_real * kernel_real - spectrum_imag * kernel_imag
        product_imag = spectrum_real * kernel_imag + spectrum_imag * kernel_real
        stacked = jnp.concatenate([product_real, product_imag[1:half_steps]], axis=0) * row_weight
        smoothed = lax.dot_general(
            forward,
            stacked,
            (((0,), (0,)), ((), ())),
            precision=lax.Precision.HIGHEST,
            preferred_element_type=jnp.float32,
        )
        power_cols = jnp.clip(smoothed, -my_cap[None, :], my_cap[None, :])
        power_time = lax.all_to_all(power_cols, TM, split_axis=0, concat_axis=1, tiled=True)
    entries = float(horizon * line_limit.shape[0] * area_devices)
    summed = lax.psum(jnp.stack(totals), TM_AREA)
    primal_rms = jnp.sqrt(summed / entries)
    return (power_time, line_duals, primal_rms)


def solution(mesh):
    finer = Mesh(mesh.devices.reshape(16, 4, 4, 2), ("tm_0", "tm_1", "area_0", "area_1"))
    placed = (
        P(TM, AREA),
        P(TM, AREA),
        P(AREA, None, None),
        P(),
        P(),
        P(),
        P(AREA),
        P(AREA),
        P(AREA),
        P(AREA),
        P(),
    )
    return jax.shard_map(
        per_device,
        mesh=finer,
        in_specs=placed,
        out_specs=(P(TM, AREA), P(TM, AREA), P()),
        check_vma=False,
    )
```

profile of v0, /device:TPU:8, one launch (start us, length us, event | category | flops | bytes accessed | tf_op | source)
XLA Modules:
  0.0 396.6 jit_solution(17762997398970816326)
XLA Ops:
  0.7 1.1 convert_element_type.36
  1.7 1.0 broadcast_in_dim.55
  2.7 4.3 %all-to-all-start = ((bf16[8,4,8960]{2,1,0:T(4,128)(2,1)}), bf16[8,4,8960]{2,1,0:T(4,128)(2,1)S(1)}, u32[]{:S(2)}, u32[]{:S(2)}) async-start(bf16[8,4,8960]{2,1,0:T(4,128)(2,1)} %broadcast_in_dim.55), calls=%async_computation | async-start | bytes 1146880 | tf_op jit(solution)/shard_map/all_to_all | solution.py:25
  7.0 0.5 broadcast.367
  7.5 1.3 reduce.5
  8.9 0.8 mul.125
  9.7 0.2 convert_reduce_fusion
  9.9 0.8 reshape.267
  10.7 0.7 fusion.85
  12.0 0.8 dynamic_slice.20
  12.8 0.8 compare_and_fusion
  13.6 0.8 compare_select_fusion
  14.3 3.5 all-to-all-done
  17.8 0.6 gather_fusion
  18.4 0.5 fusion.27
  19.0 1.7 scatter_fusion
  20.7 0.6 gather_fusion.1
  21.3 0.4 fusion.36
  21.7 0.7 broadcast.222.clone
  22.4 3.7 scatter_fusion.1
  26.1 3.4 all-to-all-start.1
  29.5 6.7 %all-to-all-done.1 = f32[4,8,6,256]{3,0,2,1:T(4,128)S(1)} async-done(((f32[4,8,6,256]{3,0,2,1:T(4,128)}), f32[4,8,6,256]{3,0,2,1:T(4,128)S(1)}, u32[]{:S(2)}, u32[]{:S(2)}) %all-to-all-start.1) | async-done | bytes 196640 | tf_op jit(solution)/shard_map/all_to_all | solution.py:149
  36.2 2.4 scatter_fusion.2
  38.6 2.8 copy.80
  41.4 30.0 %gather_fusion.2 = f32[8192,4]{1,0:T(8,128)} fusion(f32[4,8960]{0,1:T(8,128)} %copy.80, s32[8192]{0:T(1024)S(1)} %get-tuple-element.26), kind=kCustom, calls=%fused_computation.2.clone | custom fusion | bytes 294912 | tf_op jit(solution)/shard_map/jit(_take)/gather | solution.py:156
  71.4 2.8 copy.81
  74.3 0.7 fusion.17
  75.0 18.7 %all-to-all-start.2 = ((f32[4,64,128]{2,0,1:T(4,128)}), f32[4,64,128]{2,0,1:T(4,128)S(1)}, u32[]{:S(2)}, u32[]{:S(2)}) async-start(f32[4,64,128]{2,0,1:T(4,128)} %fusion.17), calls=%async_computation.2 | async-start | bytes 262144 | tf_op jit(solution)/shard_map/all_to_all | solution.py:158
  93.8 1.7 fusion.19
  95.4 0.3 fusion.49
  95.8 0.8 fusion.84
  96.5 13.5 %all-to-all-done.2 = f32[4,64,128]{2,0,1:T(4,128)S(1)} async-done(((f32[4,64,128]{2,0,1:T(4,128)}), f32[4,64,128]{2,0,1:T(4,128)S(1)}, u32[]{:S(2)}, u32[]{:S(2)}) %all-to-all-start.2) | async-done | bytes 131104 | tf_op jit(solution)/shard_map/all_to_all | solution.py:158
  110.0 2.2 fusion.20
  112.3 2.3 fusion.1
  114.7 5.6 %all-to-all-start.3 = ((f32[64,4,128]{2,1,0:T(4,128)}), f32[64,4,128]{2,1,0:T(4,128)S(1)}, u32[]{:S(2)}, u32[]{:S(2)}) async-start(f32[64,4,128]{2,1,0:T(4,128)} %bitcast.23), calls=%async_computation.3 | async-start | bytes 262144 | tf_op jit(solution)/shard_map/all_to_all | solution.py:175
  120.3 2.8 copy.83
  123.1 12.8 %all-to-all-done.3 = f32[64,4,128]{2,1,0:T(4,128)S(1)} async-done(((f32[64,4,128]{2,1,0:T(4,128)}), f32[64,4,128]{2,1,0:T(4,128)S(1)}, u32[]{:S(2)}, u32[]{:S(2)}) %all-to-all-start.3) | async-done | bytes 131104 | tf_op jit(solution)/shard_map/all_to_all | solution.py:175
  135.9 2.7 copy.84
  138.6 44.2 %scatter_fusion.3 = f32[4,8960]{0,1:T(8,128)} fusion(f32[4,8960]{0,1:T(8,128)} %copy.83, s32[8192]{0:T(1024)S(1)} %get-tuple-element.25, f32[8192,4]{1,0:T(8,128)} %copy.84), kind=kCustom, calls=%fused_computation.9 | custom fusion | flops 32768 | bytes 425984 | tf_op jit(solution)/shard_map/scatter-add | solution.py:118
  182.8 3.0 copy.85
  186.0 13.3 %all_to_all.96 = bf16[8,4,8960]{2,1,0:T(4,128)(2,1)S(1)} all-to-all(bf16[8,4,8960]{2,1,0:T(4,128)(2,1)S(1)} %broadcast_in_dim.60), channel_id=1, replica_groups=mesh['tm_0'=16,'tm_1'=4,'area_0'=4,'area_1'=2] {'area_0','area_1'}, dimensions={0} | all-to-all | bytes 1146880 | tf_op jit(solution)/shard_map/all_to_all | solution.py:25
  199.2 0.6 gather_fusion.3
  199.8 0.5 fusion.25
  200.4 1.7 scatter_fusion.4
  202.1 0.6 multiply_reduce_fusion.1
  202.7 0.6 gather_fusion.4
  203.3 0.4 fusion.34
  203.7 1.5 scatter_fusion.5
  205.3 9.2 %all_to_all.97 = f32[4,8,6,256]{3,0,2,1:T(4,128)S(1)} all-to-all(f32[4,8,6,256]{3,0,2,1:T(4,128)S(1)} %bitcast.125), channel_id=1, replica_groups=mesh['tm_0'=16,'tm_1'=4,'area_0'=4,'area_1'=2] {'area_0','area_1'}, dimensions={1} | all-to-all | bytes 393216 | tf_op jit(solution)/shard_map/all_to_all | solution.py:149
  214.5 2.4 scatter_fusion.6
  216.9 2.8 copy.88
  219.7 30.0 %gather_fusion.5 = f32[8192,4]{1,0:T(8,128)} fusion(f32[4,8960]{0,1:T(8,128)} %copy.88, s32[8192]{0:T(1024)S(1)} %get-tuple-element.26), kind=kCustom, calls=%fused_computation.5.clone | custom fusion | bytes 294912 | tf_op jit(solution)/shard_map/jit(_take)/gather | solution.py:156
  249.7 2.8 copy.89
  252.5 0.7 fusion.14
  253.3 5.8 %all-to-all-start.6 = ((f32[4,64,128]{2,0,1:T(4,128)}), f32[4,64,128]{2,0,1:T(4,128)S(1)}, u32[]{:S(2)}, u32[]{:S(2)}) async-start(f32[4,64,128]{2,0,1:T(4,128)} %fusion.14), calls=%async_computation.6 | async-start | bytes 262144 | tf_op jit(solution)/shard_map/all_to_all | solution.py:158
  259.1 1.4 pad_maximum_fusion.6
  260.4 102.7 %psum.7 = f32[2]{0:T(128)S(1)} all-reduce(f32[2]{0:T(128)S(1)} %pad_maximum_fusion.6), channel_id=1, replica_groups=mesh['tm_0'=16,'tm_1'=4,'area_0'=4,'area_1'=2] {'tm_0','tm_1','area_0','..., use_global_device_ids=true, to_apply=%region_12.16 | all-reduce | flops 2 | bytes 16 | tf_op jit(solution)/shard_map/psum | solution.py:177
  363.1 2.2 fusion.18
  365.4 2.3 fusion
  367.8 11.6 %all-to-all-start.7 = ((f32[64,4,128]{2,1,0:T(4,128)}), f32[64,4,128]{2,1,0:T(4,128)S(1)}, u32[]{:S(2)}, u32[]{:S(2)}) async-start(f32[64,4,128]{2,1,0:T(4,128)} %bitcast.40), calls=%async_computation.7 | async-start | bytes 262144 | tf_op jit(solution)/shard_map/all_to_all | solution.py:175
  379.4 0.5 multiply_sqrt_fusion
  379.9 0.6 minimum_subtract_fusion
  380.6 15.4 %all-to-all-done.7 = f32[64,4,128]{2,1,0:T(4,128)S(1)} async-done(((f32[64,4,128]{2,1,0:T(4,128)}), f32[64,4,128]{2,1,0:T(4,128)S(1)}, u32[]{:S(2)}, u32[]{:S(2)}) %all-to-all-start.7) | async-done | bytes 131104 | tf_op jit(solution)/shard_map/all_to_all | solution.py:175
  396.0 0.7 copy.100
  (44 shorter events, 1.2 us)
Async XLA Ops:
  0.6 17.8 %copy-start = (bf16[24,128,256]{2,1,0:T(8,128)(2,1)S(1)}, bf16[24,128,256]{2,1,0:T(8,128)(2,1)}, u32[]{:S(2)}) copy-start(bf16[24,128,256]{2,1,0:T(8,128)(2,1)} %param.19) | copy-start | bytes 4718596
  0.6 20.1 %copy-start.3 = (f32[1536]{0:T(1024)S(1)}, f32[1536]{0:T(1024)}, u32[]{:S(2)}) copy-start(f32[1536]{0:T(1024)} %param.26) | copy-start | bytes 18436
  2.7 15.1 %all-to-all-start = ((bf16[8,4,8960]{2,1,0:T(4,128)(2,1)}), bf16[8,4,8960]{2,1,0:T(4,128)(2,1)S(1)}, u32[]{:S(2)}, u32[]{:S(2)}) async-start(bf16[8,4,8960]{2,1,0:T(4,128)(2,1)} %broadcast_in_dim.55), calls=%async_computation | async-start | bytes 1146880 | tf_op jit(solution)/shard_map/all_to_all | solution.py:25
  26.1 10.1 %all-to-all-start.1 = ((f32[4,8,6,256]{3,0,2,1:T(4,128)}), f32[4,8,6,256]{3,0,2,1:T(4,128)S(1)}, u32[]{:S(2)}, u32[]{:S(2)}) async-start(f32[4,8,6,256]{3,0,2,1:T(4,128)} %bitcast.15), calls=%async_computation.1 | async-start | bytes 393216 | tf_op jit(solution)/shard_map/all_to_all | solution.py:149
  38.6 35.7 %copy-start.2 = (f32[4,8192]{1,0:T(4,128)S(1)}, f32[4,8192]{1,0:T(4,128)}, u32[]{:S(2)}) copy-start(f32[4,8192]{1,0:T(4,128)} %param.18) | copy-start | bytes 393220
  41.4 52.3 %copy-start.4 = (f32[3,256]{1,0:T(4,128)S(1)}, f32[3,256]{1,0:T(4,128)}, u32[]{:S(2)}) copy-start(f32[3,256]{1,0:T(4,128)} %param.27) | copy-start | bytes 9220
  74.3 46.0 %copy-start.1 = (f32[4,8960]{1,0:T(4,128)S(1)}, f32[4,8960]{1,0:T(4,128)}, u32[]{:S(2)}) copy-start(f32[4,8960]{1,0:T(4,128)} %param.17) | copy-start | bytes 430084
  75.0 35.0 %all-to-all-start.2 = ((f32[4,64,128]{2,0,1:T(4,128)}), f32[4,64,128]{2,0,1:T(4,128)S(1)}, u32[]{:S(2)}, u32[]{:S(2)}) async-start(f32[4,64,128]{2,0,1:T(4,128)} %fusion.17), calls=%async_computation.2 | async-start | bytes 262144 | tf_op jit(solution)/shard_map/all_to_all | solution.py:158
  114.7 21.2 %all-to-all-start.3 = ((f32[64,4,128]{2,1,0:T(4,128)}), f32[64,4,128]{2,1,0:T(4,128)S(1)}, u32[]{:S(2)}, u32[]{:S(2)}) async-start(f32[64,4,128]{2,1,0:T(4,128)} %bitcast.23), calls=%async_computation.3 | async-start | bytes 262144 | tf_op jit(solution)/shard_map/all_to_all | solution.py:175
  253.3 109.9 %all-to-all-start.6 = ((f32[4,64,128]{2,0,1:T(4,128)}), f32[4,64,128]{2,0,1:T(4,128)S(1)}, u32[]{:S(2)}, u32[]{:S(2)}) async-start(f32[4,64,128]{2,0,1:T(4,128)} %fusion.14), calls=%async_computation.6 | async-start | bytes 262144 | tf_op jit(solution)/shard_map/all_to_all | solution.py:158
  367.8 28.2 %all-to-all-start.7 = ((f32[64,4,128]{2,1,0:T(4,128)}), f32[64,4,128]{2,1,0:T(4,128)S(1)}, u32[]{:S(2)}, u32[]{:S(2)}) async-start(f32[64,4,128]{2,1,0:T(4,128)} %bitcast.40), calls=%async_computation.7 | async-start | bytes 262144 | tf_op jit(solution)/shard_map/all_to_all | solution.py:175
where the time goes:
time: 398 us; the launch traced here: 397 us
  blocking collectives  125 us (31%)
  local copies, waits for them, and re-layouts  93.1 us (23%)
  other arithmetic  63.2 us (16%)
  waiting for transfers between devices  51.9 us (13%)
  starting transfers between devices  49.4 us (12%)
  matrix products  12.9 us (3%)
    psum x1, blocking collectives, per_device(): summed = lax.psum(jnp.stack(totals), TM_AREA)  103 us
    gather x4, local copies, waits for them, and re-layouts, per_device(): gradient = unit_cost + rho_weight * jnp.take(prices, unit_bus, axis=1)  65.7 us
    scatter-add x1, other arithmetic, per_device(): injection = demand.at[:, unit_bus].add(power_time).astype(jnp.bfloat16)  44.2 us
    all_to_all x2, waiting for transfers between devices, per_device(): lax.all_to_all(power_cols, TM, split_axis=0, concat_axis=1, tiled=True)  28.2 us
    all_to_all x2, starting transfers between devices, per_device(): lax.all_to_all(target, TM, split_axis=1, concat_axis=0, tiled=True)  24.5 us
    all_to_all x2, starting transfers between devices, per_device(): lax.all_to_all(power_cols, TM, split_axis=0, concat_axis=1, tiled=True)  17.2 us
    all_to_all x2, waiting for transfers between devices, per_device(): lax.all_to_all(target, TM, split_axis=1, concat_axis=0, tiled=True)  13.5 us
    all_to_all x1, blocking collectives, copy_for_each(): lax.all_to_all(jnp.broadcast_to(array[None], (count, *array.shape)), axis...  13.3 us
  transfers between devices with their start and end apart: 6, of which 5 were waited for; matrix products, arithmetic and copies ran while one was open for 4% of the time, Pallas kernels for 0%

commit v1 on v0

--- a/solution.py
+++ b/solution.py
@@ -12,6 +12,12 @@
 TM_AREA = ("tm_0", "tm_1", "area_0", "area_1")
 step_size = 0.5
 rho_weight = 1.0
+
+
+def exchange_blocks(value, name, split, join):
+    pieces = jnp.split(value, lax.axis_size(name), axis=split)
+    received = lax.all_to_all(jnp.stack(pieces), name, 0, 0)
+    return jnp.concatenate(received, axis=join)
 
 
 def laid_out(tiles, dim):
@@ -172,7 +178,7 @@
             preferred_element_type=jnp.float32,
         )
         power_cols = jnp.clip(smoothed, -my_cap[None, :], my_cap[None, :])
-        power_time = lax.all_to_all(power_cols, TM, split_axis=0, concat_axis=1, tiled=True)
+        power_time = exchange_blocks(power_cols, TM, 0, 1)
     entries = float(horizon * line_limit.shape[0] * area_devices)
     summed = lax.psum(jnp.stack(totals), TM_AREA)
     primal_rms = jnp.sqrt(summed / entries)

time: 398 us -> 471 us (1.18)
  local copies, waits for them, and re-layouts: 93.1 us -> 167 us
    unnamed x13 -> x139, local copies, waits for them, and re-layouts: 3.99 us -> 77 us
  transfers between devices with their start and end apart: 6 -> 6, of which waited for: 5 -> 5; matrix products, arithmetic and copies ran while one was open for 4% -> 3% of each run, Pallas kernels for 0% -> 0%
where the time goes in v1:
time: 471 us; the launch traced here: 470 us
  local copies, waits for them, and re-layouts  167 us (35%)
  blocking collectives  125 us (27%)
  other arithmetic  63.2 us (13%)
  waiting for transfers between devices  51.9 us (11%)
  starting transfers between devices  49.4 us (10%)
  matrix products  11.6 us (2%)
    psum x1, blocking collectives, per_device(): summed = lax.psum(jnp.stack(totals), TM_AREA)  103 us
    unnamed x139, local copies, waits for them, and re-layouts  77 us
    gather x4, local copies, waits for them, and re-layouts, per_device(): gradient = unit_cost + rho_weight * jnp.take(prices, unit_bus, axis=1)  65.7 us
    scatter-add x1, other arithmetic, per_device(): injection = demand.at[:, unit_bus].add(power_time).astype(jnp.bfloat16)  44.2 us
    all_to_all x2, waiting for transfers between devices, exchange_blocks(): received = lax.all_to_all(jnp.stack(pieces), name, 0, 0)  28.2 us
    all_to_all x2, starting transfers between devices, per_device(): lax.all_to_all(target, TM, split_axis=1, concat_axis=0, tiled=True)  24.5 us
    all_to_all x2, starting transfers between devices, exchange_blocks(): received = lax.all_to_all(jnp.stack(pieces), name, 0, 0)  17.2 us
    all_to_all x2, waiting for transfers between devices, per_device(): lax.all_to_all(target, TM, split_axis=1, concat_axis=0, tiled=True)  13.5 us
  transfers between devices with their start and end apart: 6, of which 5 were waited for; matrix products, arithmetic and copies ran while one was open for 3% of the time, Pallas kernels for 0%

profile of v1, /device:TPU:8, one launch (start us, length us, event | category | flops | bytes accessed | tf_op | source)
XLA Modules:
  0.0 469.5 jit_solution(18356915278781812352)
XLA Ops:
  0.7 1.1 convert_element_type.36
  1.7 1.0 broadcast_in_dim.55
  2.7 4.3 all-to-all-start
  7.5 1.3 reduce.5
  8.9 0.8 mul.125
  9.9 0.8 reshape.273
  10.7 0.7 fusion.85
  12.0 0.8 dynamic_slice.20
  12.8 0.8 compare_and_fusion
  13.6 0.8 compare_select_fusion
  14.3 3.5 all-to-all-done
  17.8 0.6 gather_fusion
  19.0 1.7 scatter_fusion
  20.7 0.6 gather_fusion.1
  21.7 0.7 broadcast.222.clone
  22.4 3.7 scatter_fusion.1
  26.1 3.4 all-to-all-start.1
  29.5 6.7 %all-to-all-done.1 = f32[4,8,6,256]{3,0,2,1:T(4,128)S(1)} async-done(((f32[4,8,6,256]{3,0,2,1:T(4,128)}), f32[4,8,6,256]{3,0,2,1:T(4,128)S(1)}, u32[]{:S(2)}, u32[]{:S(2)}) %all-to-all-start.1) | async-done | bytes 196640 | tf_op jit(solution)/shard_map/all_to_all | solution.py:155
  36.2 2.4 scatter_fusion.2
  38.6 2.8 copy.62
  41.4 30.0 %gather_fusion.2 = f32[8192,4]{1,0:T(8,128)} fusion(f32[4,8960]{0,1:T(8,128)} %copy.62, s32[8192]{0:T(1024)S(1)} %get-tuple-element.26), kind=kCustom, calls=%fused_computation.2.clone | custom fusion | bytes 294912 | tf_op jit(solution)/shard_map/jit(_take)/gather | solution.py:162
  71.4 2.8 copy.63
  74.3 0.7 fusion.17
  75.0 18.7 %all-to-all-start.2 = ((f32[4,64,128]{2,0,1:T(4,128)}), f32[4,64,128]{2,0,1:T(4,128)S(1)}, u32[]{:S(2)}, u32[]{:S(2)}) async-start(f32[4,64,128]{2,0,1:T(4,128)} %fusion.17), calls=%async_computation.2 | async-start | bytes 262144 | tf_op jit(solution)/shard_map/all_to_all | solution.py:164
  93.8 1.7 fusion.19
  95.8 0.8 fusion.84
  96.5 13.5 %all-to-all-done.2 = f32[4,64,128]{2,0,1:T(4,128)S(1)} async-done(((f32[4,64,128]{2,0,1:T(4,128)}), f32[4,64,128]{2,0,1:T(4,128)S(1)}, u32[]{:S(2)}, u32[]{:S(2)}) %all-to-all-start.2) | async-done | bytes 131104 | tf_op jit(solution)/shard_map/all_to_all | solution.py:164
  110.0 2.2 fusion.20
  112.3 1.7 fusion.1
  114.0 0.6 constant_dynamic-update-slice_fusion.63
  114.6 0.6 constant_dynamic-update-slice_fusion.62
  115.8 0.6 constant_dynamic-update-slice_fusion.60
  116.9 0.6 constant_dynamic-update-slice_fusion.58
  118.1 0.6 constant_dynamic-update-slice_fusion.56
  119.2 0.6 constant_dynamic-update-slice_fusion.54
  120.4 0.6 constant_dynamic-update-slice_fusion.52
  151.1 5.6 %all-to-all-start.3 = ((f32[64,4,128]{2,1,0:T(4,128)}), f32[64,4,128]{2,1,0:T(4,128)S(1)}, u32[]{:S(2)}, u32[]{:S(2)}) async-start(f32[64,4,128]{2,1,0:T(4,128)} %constant_dynamic-update-slice_fusion), calls=%async_computation.3 | async-start | bytes 262144 | tf_op jit(solution)/shard_map/all_to_all | solution.py:19
  156.8 2.8 copy.65
  159.6 12.8 %all-to-all-done.3 = f32[64,4,128]{2,1,0:T(4,128)S(1)} async-done(((f32[64,4,128]{2,1,0:T(4,128)}), f32[64,4,128]{2,1,0:T(4,128)S(1)}, u32[]{:S(2)}, u32[]{:S(2)}) %all-to-all-start.3) | async-done | bytes 131104 | tf_op jit(solution)/shard_map/all_to_all | solution.py:19
  172.3 2.7 copy.66
  175.0 44.2 %scatter_fusion.3 = f32[4,8960]{0,1:T(8,128)} fusion(f32[4,8960]{0,1:T(8,128)} %copy.65, s32[8192]{0:T(1024)S(1)} %get-tuple-element.25, f32[8192,4]{1,0:T(8,128)} %copy.66), kind=kCustom, calls=%fused_computation.9 | custom fusion | flops 32768 | bytes 425984 | tf_op jit(solution)/shard_map/scatter-add | solution.py:124
  219.2 3.0 copy.67
  222.4 13.3 %all_to_all.68 = bf16[8,4,8960]{2,1,0:T(4,128)(2,1)S(1)} all-to-all(bf16[8,4,8960]{2,1,0:T(4,128)(2,1)S(1)} %broadcast_in_dim.60), channel_id=1, replica_groups=mesh['tm_0'=16,'tm_1'=4,'area_0'=4,'area_1'=2] {'area_0','area_1'}, dimensions={0} | all-to-all | bytes 1146880 | tf_op jit(solution)/shard_map/all_to_all | solution.py:31
  235.7 0.6 gather_fusion.3
  236.8 1.7 scatter_fusion.4
  238.6 0.6 multiply_reduce_fusion.1
  239.2 0.6 gather_fusion.4
  240.2 1.5 scatter_fusion.5
  241.7 9.2 %all_to_all.69 = f32[4,8,6,256]{3,0,2,1:T(4,128)S(1)} all-to-all(f32[4,8,6,256]{3,0,2,1:T(4,128)S(1)} %bitcast.635), channel_id=1, replica_groups=mesh['tm_0'=16,'tm_1'=4,'area_0'=4,'area_1'=2] {'area_0','area_1'}, dimensions={1} | all-to-all | bytes 393216 | tf_op jit(solution)/shard_map/all_to_all | solution.py:155
  251.0 2.4 scatter_fusion.6
  253.3 2.8 copy.70
  256.1 30.0 %gather_fusion.5 = f32[8192,4]{1,0:T(8,128)} fusion(f32[4,8960]{0,1:T(8,128)} %copy.70, s32[8192]{0:T(1024)S(1)} %get-tuple-element.26), kind=kCustom, calls=%fused_computation.5.clone | custom fusion | bytes 294912 | tf_op jit(solution)/shard_map/jit(_take)/gather | solution.py:162
  286.1 2.8 copy.71
  289.0 0.7 fusion.14
  289.7 5.8 %all-to-all-start.6 = ((f32[4,64,128]{2,0,1:T(4,128)}), f32[4,64,128]{2,0,1:T(4,128)S(1)}, u32[]{:S(2)}, u32[]{:S(2)}) async-start(f32[4,64,128]{2,0,1:T(4,128)} %fusion.14), calls=%async_computation.6 | async-start | bytes 262144 | tf_op jit(solution)/shard_map/all_to_all | solution.py:164
  295.5 1.4 pad_maximum_fusion.6
  296.9 102.7 %psum.7 = f32[2]{0:T(128)S(1)} all-reduce(f32[2]{0:T(128)S(1)} %pad_maximum_fusion.6), channel_id=1, replica_groups=mesh['tm_0'=16,'tm_1'=4,'area_0'=4,'area_1'=2] {'tm_0','tm_1','area_0','..., use_global_device_ids=true, to_apply=%region_12.16 | all-reduce | flops 2 | bytes 16 | tf_op jit(solution)/shard_map/psum | solution.py:183
  399.6 2.2 fusion.18
  401.9 1.7 fusion
  403.6 0.6 constant_dynamic-update-slice_fusion.127
  440.7 11.6 %all-to-all-start.7 = ((f32[64,4,128]{2,1,0:T(4,128)}), f32[64,4,128]{2,1,0:T(4,128)S(1)}, u32[]{:S(2)}, u32[]{:S(2)}) async-start(f32[64,4,128]{2,1,0:T(4,128)} %constant_dynamic-update-slice_fusion.64), calls=%async_computation.7 | async-start | bytes 262144 | tf_op jit(solution)/shard_map/all_to_all | solution.py:19
  452.8 0.6 minimum_subtract_fusion
  453.5 15.4 %all-to-all-done.7 = f32[64,4,128]{2,1,0:T(4,128)S(1)} async-done(((f32[64,4,128]{2,1,0:T(4,128)}), f32[64,4,128]{2,1,0:T(4,128)S(1)}, u32[]{:S(2)}, u32[]{:S(2)}) %all-to-all-start.7) | async-done | bytes 131104 | tf_op jit(solution)/shard_map/all_to_all | solution.py:19
  468.9 0.7 copy.207
  (172 shorter events, 74.1 us)
Async XLA Ops:
  0.6 17.8 %copy-start = (bf16[24,128,256]{2,1,0:T(8,128)(2,1)S(1)}, bf16[24,128,256]{2,1,0:T(8,128)(2,1)}, u32[]{:S(2)}) copy-start(bf16[24,128,256]{2,1,0:T(8,128)(2,1)} %param.19) | copy-start | bytes 4718596
  0.6 20.1 %copy-start.3 = (f32[1536]{0:T(1024)S(1)}, f32[1536]{0:T(1024)}, u32[]{:S(2)}) copy-start(f32[1536]{0:T(1024)} %param.26) | copy-start | bytes 18436
  2.7 15.1 %all-to-all-start = ((bf16[8,4,8960]{2,1,0:T(4,128)(2,1)}), bf16[8,4,8960]{2,1,0:T(4,128)(2,1)S(1)}, u32[]{:S(2)}, u32[]{:S(2)}) async-start(bf16[8,4,8960]{2,1,0:T(4,128)(2,1)} %broadcast_in_dim.55), calls=%async_computation | async-start | bytes 1146880 | tf_op jit(solution)/shard_map/all_to_all | solution.py:31
  26.1 10.1 %all-to-all-start.1 = ((f32[4,8,6,256]{3,0,2,1:T(4,128)}), f32[4,8,6,256]{3,0,2,1:T(4,128)S(1)}, u32[]{:S(2)}, u32[]{:S(2)}) async-start(f32[4,8,6,256]{3,0,2,1:T(4,128)} %bitcast.15), calls=%async_computation.1 | async-start | bytes 393216 | tf_op jit(solution)/shard_map/all_to_all | solution.py:155
  38.6 35.7 %copy-start.2 = (f32[4,8192]{1,0:T(4,128)S(1)}, f32[4,8192]{1,0:T(4,128)}, u32[]{:S(2)}) copy-start(f32[4,8192]{1,0:T(4,128)} %param.18) | copy-start | bytes 393220
  41.4 52.3 %copy-start.4 = (f32[3,256]{1,0:T(4,128)S(1)}, f32[3,256]{1,0:T(4,128)}, u32[]{:S(2)}) copy-start(f32[3,256]{1,0:T(4,128)} %param.27) | copy-start | bytes 9220
  74.3 82.5 %copy-start.1 = (f32[4,8960]{1,0:T(4,128)S(1)}, f32[4,8960]{1,0:T(4,128)}, u32[]{:S(2)}) copy-start(f32[4,8960]{1,0:T(4,128)} %param.17) | copy-start | bytes 430084
  75.0 35.0 %all-to-all-start.2 = ((f32[4,64,128]{2,0,1:T(4,128)}), f32[4,64,128]{2,0,1:T(4,128)S(1)}, u32[]{:S(2)}, u32[]{:S(2)}) async-start(f32[4,64,128]{2,0,1:T(4,128)} %fusion.17), calls=%async_computation.2 | async-start | bytes 262144 | tf_op jit(solution)/shard_map/all_to_all | solution.py:164
  151.1 21.2 %all-to-all-start.3 = ((f32[64,4,128]{2,1,0:T(4,128)}), f32[64,4,128]{2,1,0:T(4,128)S(1)}, u32[]{:S(2)}, u32[]{:S(2)}) async-start(f32[64,4,128]{2,1,0:T(4,128)} %constant_dynamic-update-slice_fusion), calls=%async_computation.3 | async-start | bytes 262144 | tf_op jit(solution)/shard_map/all_to_all | solution.py:19
  289.7 109.9 %all-to-all-start.6 = ((f32[4,64,128]{2,0,1:T(4,128)}), f32[4,64,128]{2,0,1:T(4,128)S(1)}, u32[]{:S(2)}, u32[]{:S(2)}) async-start(f32[4,64,128]{2,0,1:T(4,128)} %fusion.14), calls=%async_computation.6 | async-start | bytes 262144 | tf_op jit(solution)/shard_map/all_to_all | solution.py:164
  440.7 28.2 %all-to-all-start.7 = ((f32[64,4,128]{2,1,0:T(4,128)}), f32[64,4,128]{2,1,0:T(4,128)S(1)}, u32[]{:S(2)}, u32[]{:S(2)}) async-start(f32[64,4,128]{2,1,0:T(4,128)} %constant_dynamic-update-slice_fusion.64), calls=%async_computation.7 | async-start | bytes 262144 | tf_op jit(solution)/shard_map/all_to_all | solution.py:19
